TPU v7x, 256 devices: a whole 4x4x8 slice. The times are simulated.
256 devices in a mesh: ctx: 64 (over y, z_lo, x), tp: 4 (over z_hi, core).
Axes of the slice: x: 4, y: 4, z: 8 (z_hi: 2, z_lo: 4; z = z_hi * 4 + z_lo), core: 2. Of those that a mesh axis runs over, the one named last changes fastest.
Arguments:
- activations: bfloat16 [40960, 4096], P('ctx', 'tp'), may hold values from -6 to 6
- group_counts: int32 [64], replicated, may hold values from 1 to 5, as said below
- genome_starts: int32 [32], replicated, may hold values from 0 to 24448, as said below
- in_weight: bfloat16 [4096, 3, 2048], P('ctx', None, 'tp'), may hold values from -0.09375 to 0.09375
- short_taps: float32 [7, 3, 2048], P(None, None, 'tp'), may hold values from -2 to 2
- long_taps: float32 [128, 2048], P(None, 'tp'), may hold values from -0.5 to 0.5
- out_weight: bfloat16 [2048, 4096], P('tp', 'ctx'), may hold values from -0.125 to 0.125
Outputs:
- block_out: bfloat16 [40960, 4096], P('ctx', 'tp')
Inputs may be any that keep to these rules, and one draw needn't show every extreme that they name: Every device holds 1 or more blocks; group_counts[2k] + group_counts[2k+1] = 6 for every k. `genome_starts`: strictly increasing; the first entry is 0 and the last is exactly 24448.
All inputs are finite; a program needn't handle non-finite values.
Results may differ from a plain program's by a relative error of at most 0.012.
Values may be sent and summed in bfloat16 or wider, within the bound.
No kernel may reach another device: no remote copies, remote signals or barrier semaphores. Data moves between devices by JAX's collectives and lax.ppermute only.
A program may use at most 128 MiB of HBM per device.

v0:
```python
import jax
import jax.numpy as jnp
from jax import lax
from jax.sharding import PartitionSpec as P

GROUP = 128


def passed_along(shard, axis, by):
    peers = lax.axis_size(axis)
    pairs = [(i, i + by) for i in range(peers) if 0 <= i + by < peers]
    return lax.ppermute(shard, axis, pairs)


def genome_start(positions, genome_starts):
    above = genome_starts[None, :] <= positions[:, None]
    return jnp.max(jnp.where(above, genome_starts[None, :], 0), axis=1)


def causal_taps(padded, taps, positions, gstart, width):
    count = positions.shape[0]
    shape = (count,) + (1,) * (padded.ndim - 1)
    summed = jnp.zeros((count,) + padded.shape[1:], jnp.float32)
    for j in range(width):
        in_genome = (positions - j >= gstart).reshape(shape)
        window = padded[width - 1 - j : width - 1 - j + count]
        summed = summed + jnp.where(in_genome, window * taps[j], jnp.float32(0.0))
    return summed


def body(activations, group_counts, genome_starts, in_weight, short_taps, long_taps, out_weight):
    ctx_size = lax.axis_size("ctx")
    my_index = lax.axis_index("ctx")
    own_rows = activations.shape[0]
    device_ids = jnp.arange(ctx_size, dtype=jnp.int32)
    own_count = jnp.sum(jnp.where(device_ids == my_index, group_counts, 0))
    offset = jnp.sum(jnp.where(device_ids < my_index, group_counts, 0))
    row_ids = jnp.arange(own_rows, dtype=jnp.int32)
    positions = offset * GROUP + row_ids
    tail_end = own_count * GROUP

    def last_rows(source, count):
        return lax.dynamic_slice_in_dim(source, tail_end - count, count, 0)

    gstart = genome_start(positions, genome_starts)
    all_feats = lax.all_gather(activations, "tp", axis=1, tiled=True)
    widened = all_feats.astype(jnp.float32)
    normed = (
        widened * lax.rsqrt(jnp.mean(widened * widened, axis=1, keepdims=True) + 1e-06)
    ).astype(jnp.bfloat16)
    row_count = normed.shape[0]
    branches = in_weight.shape[1]
    chans = in_weight.shape[2]
    shard_rows = lax.all_gather(in_weight, "ctx", axis=0, tiled=True)
    flat = shard_rows.reshape(shard_rows.shape[0], branches * chans)
    summed = jnp.dot(normed, flat, preferred_element_type=jnp.float32)
    projected = summed.astype(jnp.bfloat16).reshape(row_count, branches, chans)
    rim_short = passed_along(last_rows(projected, 6), "ctx", 1)
    feat = causal_taps(
        jnp.concatenate([rim_short, projected], axis=0).astype(jnp.float32),
        short_taps,
        positions,
        gstart,
        7,
    )
    mixed = (feat[:, 1] * feat[:, 2]).astype(jnp.bfloat16)
    rim_long = passed_along(last_rows(mixed, 127), "ctx", 1)
    filtered = causal_taps(
        jnp.concatenate([rim_long, mixed], axis=0).astype(jnp.float32),
        long_taps,
        positions,
        gstart,
        128,
    )
    gated = (feat[:, 0] * filtered).astype(jnp.bfloat16)
    partial_out = jnp.dot(
        gated,
        lax.all_gather(out_weight, "ctx", axis=1, tiled=True),
        preferred_element_type=jnp.float32,
    )
    branch_out = lax.psum_scatter(
        partial_out.astype(jnp.bfloat16), "tp", scatter_dimension=1, tiled=True
    ).astype(jnp.float32)
    result = (activations.astype(jnp.float32) + branch_out).astype(jnp.bfloat16)
    slot_ids = jnp.arange(own_rows, dtype=jnp.int32)
    live_rows = (slot_ids < own_count * GROUP)[:, None]
    return jnp.where(live_rows, result, jnp.zeros_like(result))


def solution(mesh):
    placed = (
        P("ctx", "tp"),
        P(),
        P(),
        P("ctx", None, "tp"),
        P(None, None, "tp"),
        P(None, "tp"),
        P("tp", "ctx"),
    )
    return jax.shard_map(
        body, mesh=mesh, in_specs=placed, out_specs=P("ctx", "tp"), check_vma=False
    )
```

profile of v0, /device:TPU:1, one launch (start us, length us, event | category | flops | bytes accessed | tf_op | source)
XLA Modules:
  0.0 921.4 jit_solution(7368510152280378375)
XLA Ops:
  6.6 0.7 all-gather.4.cloned.1.call-update
  7.3 0.7 all-gather.6.cloned.1.call-update
  8.1 0.7 all-gather.8.cloned.1.call-update
  9.1 0.6 fusion.283
  11.2 1.3 add_compare_fusion.95
  12.5 79.1 %all-gather.4.cloned.1.call-done = bf16[640,4096]{1,0:T(8,128)(2,1)} async-done(((bf16[640,1024]{1,0:T(8,128)(2,1)}), bf16[640,4096]{1,0:T(8,128)(2,1)}) %all-gather.4.cloned.1.call-update) | async-done | bytes 5242896 | tf_op jit(solution)/shard_map/all_gather | solution.py:46
  91.6 3.6 fusion
  95.2 321.5 %all-gather.6.cloned.1.call-done = bf16[4096,3,512]{2,0,1:T(8,128)(2,1)} async-done(((bf16[64,3,512]{2,0,1:T(8,128)(2,1)}), bf16[4096,3,512]{2,0,1:T(8,128)(2,1)}) %all-gather.6.cloned.1.call-update) | async-done | bytes 12582928 | tf_op jit(solution)/shard_map/all_gather | solution.py:54
  416.7 17.0 %copy.21 = bf16[4096,3,512]{0,2,1:T(8,128)(2,1)} copy(bf16[4096,3,512]{2,0,1:T(8,128)(2,1)} %all-gather.6.cloned.1.call-done) | data formatting | bytes 25165824 | tf_op jit(solution)/shard_map/all_gather | solution.py:54
  433.7 13.9 %fusion.18 = bf16[640,1536]{1,0:T(8,128)(2,1)} fusion(bf16[4096,1536]{0,1:T(8,128)(2,1)} %bitcast.161, bf16[640,4096]{1,0:T(8,128)(2,1)} %all-gather.4.cloned.1.call-done, f32[640]{0:T(1024)S(1)} %add_rsqrt_fusion), kind=kOutput, calls=%fused_computation.27 | convolution fusion | flops 8061911040 | bytes 19794432 | tf_op jit(solution)/shard_map/dot_general | solution.py:56
  447.6 2.8 copy.22
  450.6 1.3 collective-permute-start
  451.9 5.6 collective-permute-done
  457.5 1.0 maximum_convert_fusion
  458.6 8.1 fusion.6
  466.9 4.0 collective-permute-start.1
  471.0 1.9 collective-permute-done.1
  473.0 0.4 maximum_convert_fusion.1
  473.8 15.7 %fusion.217 = f32[640,512]{0,1:T(8,128)S(1)} fusion(f32[767,512]{0,1:T(8,128)S(1)} %maximum_convert_fusion.1, f32[512]{0:T(512)S(1)} %bitcast.178, f32[512]{0:T(512)S(1)} %bitcast.179, f32[512]{0:T(512)S(1)} %bitcast.180, f32[512]{0:T(512)S(1)} %bitcast.181, f32[512]{0:T(512)S(1)} %bitcast.182, f32[512]{0:T(512)S(1)} %bitcast.183, f32[512]{0:T(512)S(1)} %bitcast.184, ...), kind=kLoop, calls=%fused_computation.323 | loop fusion | flops 31129600 | bytes 43339776 | tf_op jit(solution)/shard_map/add | solution.py:27
  489.9 47.7 %fusion.299 = bf16[640,512]{0,1:T(8,128)(2,1)S(1)} fusion(f32[767,512]{0,1:T(8,128)S(1)} %maximum_convert_fusion.1, f32[640,512]{0,1:T(8,128)S(1)} %fusion.217, f32[512]{0:T(512)S(1)} %bitcast.197, f32[512]{0:T(512)S(1)} %bitcast.292, f32[512]{0:T(512)S(1)} %bitcast.237, f32[512]{0:T(512)S(1)} %bitcast.238, f32[512]{0:T(512)S(1)} %bitcast.239, ...), kind=kLoop, calls=%fused_computation.35.clone.clone.1 | loop fusion | flops 95027200 | bytes 129363968 | tf_op jit(solution)/shard_map/dot_general | solution.py:76
  537.6 228.4 %all-gather.8.cloned.1.call-done = bf16[512,4096]{0,1:T(8,128)(2,1)} async-done(((bf16[512,64]{0,1:T(8,128)(2,1)}), bf16[512,4096]{0,1:T(8,128)(2,1)}) %all-gather.8.cloned.1.call-update) | async-done | bytes 4194320 | tf_op jit(solution)/shard_map/all_gather | solution.py:78
  766.1 7.5 convolution_convert_fusion
  773.6 138.5 %reduce-scatter.2.cloned.1.call-done = bf16[640,1024]{1,0:T(8,128)(2,1)} async-done(((bf16[640,4096]{1,0:T(8,128)(2,1)}), bf16[640,1024]{1,0:T(8,128)(2,1)}) %reduce-scatter.2.cloned.1.call-update) | async-done | bytes 1310736 | tf_op jit(solution)/shard_map/reduce_scatter | solution.py:81
  912.0 2.8 fusion.21
  (115 shorter events, 1.3 us)
Async XLA Ops:
  6.5 85.1 %all-gather.4.cloned.1.call-start = ((), (), s32[]{:S(2)}) async-start(), calls=%async_computation.1 | async-start | bytes 6553600 | tf_op jit(solution)/shard_map/all_gather | solution.py:46
  7.3 409.5 %all-gather.6.cloned.1.call-start = ((), (), s32[]{:S(2)}) async-start(), calls=%async_computation.2 | async-start | bytes 12779520 | tf_op jit(solution)/shard_map/all_gather | solution.py:54
  8.0 758.1 %all-gather.8.cloned.1.call-start = ((), (), s32[]{:S(2)}) async-start(), calls=%async_computation.3 | async-start | bytes 4259840 | tf_op jit(solution)/shard_map/all_gather | solution.py:78
  8.8 903.3 %reduce-scatter.2.cloned.1.call-start = ((), (), s32[]{:S(2)}) async-start(), calls=%async_computation.4 | async-start | bytes 6553600 | tf_op jit(solution)/shard_map/reduce_scatter | solution.py:81
  450.6 7.0 collective-permute-start
  466.9 6.1 collective-permute-start.1
  473.3 16.1 %copy-start.3 = (pred[640]{0:T(1024)(128)(4,1)S(1)}, pred[640]{0:T(1024)(128)(4,1)}, u32[]{:S(2)}) copy-start(pred[640]{0:T(1024)(128)(4,1)} %get-tuple-element.160) | copy-start | bytes 1924
  473.4 16.1 %copy-start.4 = (pred[640]{0:T(1024)(128)(4,1)S(1)}, pred[640]{0:T(1024)(128)(4,1)}, u32[]{:S(2)}) copy-start(pred[640]{0:T(1024)(128)(4,1)} %get-tuple-element.161) | copy-start | bytes 1924
  473.4 16.1 %copy-start.5 = (pred[640]{0:T(1024)(128)(4,1)S(1)}, pred[640]{0:T(1024)(128)(4,1)}, u32[]{:S(2)}) copy-start(pred[640]{0:T(1024)(128)(4,1)} %get-tuple-element.162) | copy-start | bytes 1924
  473.4 16.1 %copy-start.6 = (pred[640]{0:T(1024)(128)(4,1)S(1)}, pred[640]{0:T(1024)(128)(4,1)}, u32[]{:S(2)}) copy-start(pred[640]{0:T(1024)(128)(4,1)} %get-tuple-element.163) | copy-start | bytes 1924
  473.4 16.1 %copy-start.7 = (pred[640]{0:T(1024)(128)(4,1)S(1)}, pred[640]{0:T(1024)(128)(4,1)}, u32[]{:S(2)}) copy-start(pred[640]{0:T(1024)(128)(4,1)} %get-tuple-element.164) | copy-start | bytes 1924
  473.4 16.1 %copy-start.8 = (pred[640]{0:T(1024)(128)(4,1)S(1)}, pred[640]{0:T(1024)(128)(4,1)}, u32[]{:S(2)}) copy-start(pred[640]{0:T(1024)(128)(4,1)} %get-tuple-element.165) | copy-start | bytes 1924
  473.4 16.1 %copy-start.9 = (pred[640]{0:T(1024)(128)(4,1)S(1)}, pred[640]{0:T(1024)(128)(4,1)}, u32[]{:S(2)}) copy-start(pred[640]{0:T(1024)(128)(4,1)} %get-tuple-element.166) | copy-start | bytes 1924
  473.4 16.1 %copy-start.10 = (pred[640]{0:T(1024)(128)(4,1)S(1)}, pred[640]{0:T(1024)(128)(4,1)}, u32[]{:S(2)}) copy-start(pred[640]{0:T(1024)(128)(4,1)} %get-tuple-element.167) | copy-start | bytes 1924
  473.4 16.1 %copy-start.11 = (pred[640]{0:T(1024)(128)(4,1)S(1)}, pred[640]{0:T(1024)(128)(4,1)}, u32[]{:S(2)}) copy-start(pred[640]{0:T(1024)(128)(4,1)} %get-tuple-element.168) | copy-start | bytes 1924
  473.4 16.1 %copy-start.12 = (pred[640]{0:T(1024)(128)(4,1)S(1)}, pred[640]{0:T(1024)(128)(4,1)}, u32[]{:S(2)}) copy-start(pred[640]{0:T(1024)(128)(4,1)} %get-tuple-element.169) | copy-start | bytes 1924
  473.5 16.1 %copy-start.13 = (pred[640]{0:T(1024)(128)(4,1)S(1)}, pred[640]{0:T(1024)(128)(4,1)}, u32[]{:S(2)}) copy-start(pred[640]{0:T(1024)(128)(4,1)} %get-tuple-element.170) | copy-start | bytes 1924
  473.5 16.1 %copy-start.14 = (pred[640]{0:T(1024)(128)(4,1)S(1)}, pred[640]{0:T(1024)(128)(4,1)}, u32[]{:S(2)}) copy-start(pred[640]{0:T(1024)(128)(4,1)} %get-tuple-element.171) | copy-start | bytes 1924
  473.5 16.1 %copy-start.15 = (pred[640]{0:T(1024)(128)(4,1)S(1)}, pred[640]{0:T(1024)(128)(4,1)}, u32[]{:S(2)}) copy-start(pred[640]{0:T(1024)(128)(4,1)} %get-tuple-element.172) | copy-start | bytes 1924
  473.5 16.1 %copy-start.16 = (pred[640]{0:T(1024)(128)(4,1)S(1)}, pred[640]{0:T(1024)(128)(4,1)}, u32[]{:S(2)}) copy-start(pred[640]{0:T(1024)(128)(4,1)} %get-tuple-element.173) | copy-start | bytes 1924
  473.5 16.1 %copy-start.17 = (pred[640]{0:T(1024)(128)(4,1)S(1)}, pred[640]{0:T(1024)(128)(4,1)}, u32[]{:S(2)}) copy-start(pred[640]{0:T(1024)(128)(4,1)} %get-tuple-element.174) | copy-start | bytes 1924
  473.5 16.1 %copy-start.18 = (pred[640]{0:T(1024)(128)(4,1)S(1)}, pred[640]{0:T(1024)(128)(4,1)}, u32[]{:S(2)}) copy-start(pred[640]{0:T(1024)(128)(4,1)} %get-tuple-element.175) | copy-start | bytes 1924
  473.5 16.1 %copy-start.19 = (pred[640]{0:T(1024)(128)(4,1)S(1)}, pred[640]{0:T(1024)(128)(4,1)}, u32[]{:S(2)}) copy-start(pred[640]{0:T(1024)(128)(4,1)} %get-tuple-element.176) | copy-start | bytes 1924
  773.5 138.5 %copy-start = (bf16[640,1024]{1,0:T(8,128)(2,1)S(1)}, bf16[640,1024]{1,0:T(8,128)(2,1)}, u32[]{:S(2)}) copy-start(bf16[640,1024]{1,0:T(8,128)(2,1)} %param.7) | copy-start | bytes 3932164
  (27 other events, 385.2 us)
Sparse Core Ops, SparseCore 0:
  9.2 82.4 all-gather.3
  93.4 323.2 all-gather.5
  418.5 347.5 all-gather.7
  773.7 138.3 reduce-scatter.1
where the time goes:
time: 922 us; the launch traced here: 921 us
  waiting for transfers between devices  777 us (84%)
  other arithmetic  81.6 us (9%)
  matrix products  21.4 us (2%)
  local copies, waits for them, and re-layouts  20.5 us (2%)
  between operations  15.3 us (2%)
    all_gather x1, waiting for transfers between devices, body(): shard_rows = lax.all_gather(in_weight, 'ctx', axis=0, tiled=True)  322 us
    all_gather x1, waiting for transfers between devices, body(): lax.all_gather(out_weight, 'ctx', axis=1, tiled=True)  228 us
    reduce_scatter x1, waiting for transfers between devices, body(): lax.psum_scatter(partial_out.astype(jnp.bfloat16), 'tp', scatter_dimensio...  138 us
    all_gather x1, waiting for transfers between devices, body(): all_feats = lax.all_gather(activations, 'tp', axis=1, tiled=True)  79.1 us
    dot_general x1, other arithmetic, body(): jnp.dot(gated, lax.all_gather(out_weight, 'ctx', axis=1, tiled=True), pre...  47.7 us
    add x2, other arithmetic, causal_taps(): summed = summed + jnp.where(in_genome, window * taps[j], jnp.float32(0.0))  23.8 us
  transfers between devices with their start and end apart: 6, of which 6 were waited for; matrix products, arithmetic and copies ran while one was open for 12% of the time, Pallas kernels for 0%

commit v1 on v0

--- a/solution.py
+++ b/solution.py
@@ -43,7 +43,9 @@
         return lax.dynamic_slice_in_dim(source, tail_end - count, count, 0)
 
     gstart = genome_start(positions, genome_starts)
-    all_feats = lax.all_gather(activations, "tp", axis=1, tiled=True)
+    all_feats = jnp.concatenate(
+        lax.all_to_all(jnp.stack([activations] * lax.axis_size("tp")), "tp", 0, 0), axis=1
+    )
     widened = all_feats.astype(jnp.float32)
     normed = (
         widened * lax.rsqrt(jnp.mean(widened * widened, axis=1, keepdims=True) + 1e-06)

time: 922 us -> 887 us (0.962)
  waiting for transfers between devices: 777 us -> 722 us
  starting transfers between devices: 5.46 us -> 15.4 us
    all_to_all x0 -> x1, waiting for transfers between devices: none -> 157 us  [body(): lax.all_to_all(jnp.stack([activations] * lax.axis_size('tp')), 'tp', 0, 0)]
    all_gather x1, waiting for transfers between devices: 322 us -> 200 us  [body(): shard_rows = lax.all_gather(in_weight, 'ctx', axis=0, tiled=True)]
    all_gather x1 -> x0, waiting for transfers between devices: 79.1 us -> none  [body(): all_feats = lax.all_gather(activations, 'tp', axis=1, tiled=True)]
    all_to_all x0 -> x1, starting transfers between devices: none -> 10.1 us  [body(): lax.all_to_all(jnp.stack([activations] * lax.axis_size('tp')), 'tp', 0, 0)]
    all_gather x1, waiting for transfers between devices: 228 us -> 219 us  [body(): lax.all_gather(out_weight, 'ctx', axis=1, tiled=True)]
  transfers between devices with their start and end apart: 6 -> 6, of which waited for: 6 -> 6; matrix products, arithmetic and copies ran while one was open for 12% -> 14% of each run, Pallas kernels for 0% -> 0%
where the time goes in v1:
time: 887 us; the launch traced here: 886 us
  waiting for transfers between devices  722 us (81%)
  other arithmetic  87.5 us (10%)
  local copies, waits for them, and re-layouts  24.9 us (3%)
  matrix products  21.3 us (2%)
  starting transfers between devices  15.4 us (2%)
  between operations  15.2 us (2%)
    all_gather x1, waiting for transfers between devices, body(): lax.all_gather(out_weight, 'ctx', axis=1, tiled=True)  219 us
    all_gather x1, waiting for transfers between devices, body(): shard_rows = lax.all_gather(in_weight, 'ctx', axis=0, tiled=True)  200 us
    all_to_all x1, waiting for transfers between devices, body(): lax.all_to_all(jnp.stack([activations] * lax.axis_size('tp')), 'tp', 0, 0)  157 us
    reduce_scatter x1, waiting for transfers between devices, body(): lax.psum_scatter(partial_out.astype(jnp.bfloat16), 'tp', scatter_dimensio...  138 us
    dot_general x1, other arithmetic, body(): jnp.dot(gated, lax.all_gather(out_weight, 'ctx', axis=1, tiled=True), pre...  47.7 us
    add x2, other arithmetic, causal_taps(): summed = summed + jnp.where(in_genome, window * taps[j], jnp.float32(0.0))  23.8 us
  transfers between devices with their start and end apart: 6, of which 6 were waited for; matrix products, arithmetic and copies ran while one was open for 14% of the time, Pallas kernels for 0%

profile of v1, /device:TPU:1, one launch (start us, length us, event | category | flops | bytes accessed | tf_op | source)
XLA Modules:
  0.0 886.5 jit_solution(1127656682145032444)
XLA Ops:
  7.3 1.7 copy.23
  9.0 2.8 stack.2
  11.8 10.1 %all-to-all-start = ((bf16[4,640,1024]{1,2,0:T(8,128)(2,1)}), bf16[4,640,1024]{1,2,0:T(8,128)(2,1)}, u32[]{:S(2)}, u32[]{:S(2)}) async-start(bf16[4,640,1024]{1,2,0:T(8,128)(2,1)} %stack.2), calls=%async_computation | async-start | bytes 10485760 | tf_op jit(solution)/shard_map/all_to_all | solution.py:47
  21.9 0.7 all-gather.5.cloned.1.call-update
  25.0 1.3 add_compare_fusion.95
  26.3 157.1 %all-to-all-done = bf16[4,640,1024]{1,2,0:T(8,128)(2,1)} async-done(((bf16[4,640,1024]{1,2,0:T(8,128)(2,1)}), bf16[4,640,1024]{1,2,0:T(8,128)(2,1)}, u32[]{:S(2)}, u32[]{:S(2)}) %all-to-all-start) | async-done | bytes 5242912 | tf_op jit(solution)/shard_map/all_to_all | solution.py:47
  183.4 3.6 fusion
  187.0 5.9 fusion.1
  192.8 200.0 %all-gather.3.cloned.1.call-done = bf16[4096,3,512]{2,0,1:T(8,128)(2,1)} async-done(((bf16[64,3,512]{2,0,1:T(8,128)(2,1)}), bf16[4096,3,512]{2,0,1:T(8,128)(2,1)}) %all-gather.3.cloned.1.call-update) | async-done | bytes 12582928 | tf_op jit(solution)/shard_map/all_gather | solution.py:56
  392.8 16.9 %copy.24 = bf16[4096,3,512]{0,2,1:T(8,128)(2,1)} copy(bf16[4096,3,512]{2,0,1:T(8,128)(2,1)} %all-gather.3.cloned.1.call-done) | data formatting | bytes 25165824 | tf_op jit(solution)/shard_map/all_gather | solution.py:56
  409.8 13.9 %convolution_convert_fusion.1 = bf16[640,1536]{1,0:T(8,128)(2,1)} fusion(bf16[640,4096]{0,1:T(8,128)(2,1)} %bitcast.168, bf16[4096,1536]{0,1:T(8,128)(2,1)} %bitcast.165), kind=kOutput, calls=%fused_computation.25 | convolution fusion | flops 8054046720 | bytes 19791872 | tf_op jit(solution)/shard_map/dot_general | solution.py:58
  423.7 2.8 copy.25
  426.6 1.5 collective-permute-start
  428.2 4.5 collective-permute-done
  432.6 1.0 maximum_convert_fusion
  433.7 8.1 fusion.3
  442.0 3.8 collective-permute-start.1
  445.9 2.2 collective-permute-done.1
  449.0 15.7 %fusion.211 = f32[640,512]{0,1:T(8,128)S(1)} fusion(f32[767,512]{0,1:T(8,128)S(1)} %maximum_convert_fusion.1, f32[512]{0:T(512)S(1)} %bitcast.183, f32[512]{0:T(512)S(1)} %bitcast.184, f32[512]{0:T(512)S(1)} %bitcast.185, f32[512]{0:T(512)S(1)} %bitcast.186, f32[512]{0:T(512)S(1)} %bitcast.187, f32[512]{0:T(512)S(1)} %bitcast.188, f32[512]{0:T(512)S(1)} %bitcast.189, ...), kind=kLoop, calls=%fused_computation.321 | loop fusion | flops 31129600 | bytes 43339776 | tf_op jit(solution)/shard_map/add | solution.py:27
  465.1 47.7 %fusion.294 = bf16[640,512]{0,1:T(8,128)(2,1)S(1)} fusion(f32[767,512]{0,1:T(8,128)S(1)} %maximum_convert_fusion.1, f32[640,512]{0,1:T(8,128)S(1)} %fusion.211, f32[512]{0:T(512)S(1)} %bitcast.202, f32[512]{0:T(512)S(1)} %bitcast.297, f32[512]{0:T(512)S(1)} %bitcast.242, f32[512]{0:T(512)S(1)} %bitcast.243, f32[512]{0:T(512)S(1)} %bitcast.244, ...), kind=kLoop, calls=%fused_computation.33.clone.clone.1 | loop fusion | flops 95027200 | bytes 129363968 | tf_op jit(solution)/shard_map/dot_general | solution.py:78
  512.9 218.5 %all-gather.5.cloned.1.call-done = bf16[512,4096]{0,1:T(8,128)(2,1)} async-done(((bf16[512,64]{0,1:T(8,128)(2,1)}), bf16[512,4096]{0,1:T(8,128)(2,1)}) %all-gather.5.cloned.1.call-update) | async-done | bytes 4194320 | tf_op jit(solution)/shard_map/all_gather | solution.py:80
  731.4 7.5 convolution_convert_fusion
  738.9 138.3 %reduce-scatter.2.cloned.1.call-done = bf16[640,1024]{1,0:T(8,128)(2,1)} async-done(((bf16[640,4096]{1,0:T(8,128)(2,1)}), bf16[640,1024]{1,0:T(8,128)(2,1)}) %reduce-scatter.2.cloned.1.call-update) | async-done | bytes 1310736 | tf_op jit(solution)/shard_map/reduce_scatter | solution.py:83
  877.2 2.8 fusion.15
  (117 shorter events, 2.9 us)
Async XLA Ops:
  6.5 386.3 %all-gather.3.cloned.1.call-start = ((), (), s32[]{:S(2)}) async-start(), calls=%async_computation.2 | async-start | bytes 12779520 | tf_op jit(solution)/shard_map/all_gather | solution.py:56
  11.8 171.6 %all-to-all-start = ((bf16[4,640,1024]{1,2,0:T(8,128)(2,1)}), bf16[4,640,1024]{1,2,0:T(8,128)(2,1)}, u32[]{:S(2)}, u32[]{:S(2)}) async-start(bf16[4,640,1024]{1,2,0:T(8,128)(2,1)} %stack.2), calls=%async_computation | async-start | bytes 10485760 | tf_op jit(solution)/shard_map/all_to_all | solution.py:47
  21.8 709.5 %all-gather.5.cloned.1.call-start = ((), (), s32[]{:S(2)}) async-start(), calls=%async_computation.3 | async-start | bytes 4259840 | tf_op jit(solution)/shard_map/all_gather | solution.py:80
  22.6 854.6 %reduce-scatter.2.cloned.1.call-start = ((), (), s32[]{:S(2)}) async-start(), calls=%async_computation.4 | async-start | bytes 6553600 | tf_op jit(solution)/shard_map/reduce_scatter | solution.py:83
  426.6 6.0 collective-permute-start
  442.0 6.2 collective-permute-start.1
  448.6 16.1 %copy-start.3 = (pred[640]{0:T(1024)(128)(4,1)S(1)}, pred[640]{0:T(1024)(128)(4,1)}, u32[]{:S(2)}) copy-start(pred[640]{0:T(1024)(128)(4,1)} %get-tuple-element.160) | copy-start | bytes 1924
  448.6 16.1 %copy-start.4 = (pred[640]{0:T(1024)(128)(4,1)S(1)}, pred[640]{0:T(1024)(128)(4,1)}, u32[]{:S(2)}) copy-start(pred[640]{0:T(1024)(128)(4,1)} %get-tuple-element.161) | copy-start | bytes 1924
  448.6 16.1 %copy-start.5 = (pred[640]{0:T(1024)(128)(4,1)S(1)}, pred[640]{0:T(1024)(128)(4,1)}, u32[]{:S(2)}) copy-start(pred[640]{0:T(1024)(128)(4,1)} %get-tuple-element.162) | copy-start | bytes 1924
  448.6 16.1 %copy-start.6 = (pred[640]{0:T(1024)(128)(4,1)S(1)}, pred[640]{0:T(1024)(128)(4,1)}, u32[]{:S(2)}) copy-start(pred[640]{0:T(1024)(128)(4,1)} %get-tuple-element.163) | copy-start | bytes 1924
  448.6 16.1 %copy-start.7 = (pred[640]{0:T(1024)(128)(4,1)S(1)}, pred[640]{0:T(1024)(128)(4,1)}, u32[]{:S(2)}) copy-start(pred[640]{0:T(1024)(128)(4,1)} %get-tuple-element.164) | copy-start | bytes 1924
  448.6 16.1 %copy-start.8 = (pred[640]{0:T(1024)(128)(4,1)S(1)}, pred[640]{0:T(1024)(128)(4,1)}, u32[]{:S(2)}) copy-start(pred[640]{0:T(1024)(128)(4,1)} %get-tuple-element.165) | copy-start | bytes 1924
  448.6 16.1 %copy-start.9 = (pred[640]{0:T(1024)(128)(4,1)S(1)}, pred[640]{0:T(1024)(128)(4,1)}, u32[]{:S(2)}) copy-start(pred[640]{0:T(1024)(128)(4,1)} %get-tuple-element.166) | copy-start | bytes 1924
  448.6 16.1 %copy-start.10 = (pred[640]{0:T(1024)(128)(4,1)S(1)}, pred[640]{0:T(1024)(128)(4,1)}, u32[]{:S(2)}) copy-start(pred[640]{0:T(1024)(128)(4,1)} %get-tuple-element.167) | copy-start | bytes 1924
  448.6 16.1 %copy-start.11 = (pred[640]{0:T(1024)(128)(4,1)S(1)}, pred[640]{0:T(1024)(128)(4,1)}, u32[]{:S(2)}) copy-start(pred[640]{0:T(1024)(128)(4,1)} %get-tuple-element.168) | copy-start | bytes 1924
  448.7 16.1 %copy-start.12 = (pred[640]{0:T(1024)(128)(4,1)S(1)}, pred[640]{0:T(1024)(128)(4,1)}, u32[]{:S(2)}) copy-start(pred[640]{0:T(1024)(128)(4,1)} %get-tuple-element.169) | copy-start | bytes 1924
  448.7 16.1 %copy-start.13 = (pred[640]{0:T(1024)(128)(4,1)S(1)}, pred[640]{0:T(1024)(128)(4,1)}, u32[]{:S(2)}) copy-start(pred[640]{0:T(1024)(128)(4,1)} %get-tuple-element.170) | copy-start | bytes 1924
  448.7 16.1 %copy-start.14 = (pred[640]{0:T(1024)(128)(4,1)S(1)}, pred[640]{0:T(1024)(128)(4,1)}, u32[]{:S(2)}) copy-start(pred[640]{0:T(1024)(128)(4,1)} %get-tuple-element.171) | copy-start | bytes 1924
  448.7 16.1 %copy-start.15 = (pred[640]{0:T(1024)(128)(4,1)S(1)}, pred[640]{0:T(1024)(128)(4,1)}, u32[]{:S(2)}) copy-start(pred[640]{0:T(1024)(128)(4,1)} %get-tuple-element.172) | copy-start | bytes 1924
  448.7 16.1 %copy-start.16 = (pred[640]{0:T(1024)(128)(4,1)S(1)}, pred[640]{0:T(1024)(128)(4,1)}, u32[]{:S(2)}) copy-start(pred[640]{0:T(1024)(128)(4,1)} %get-tuple-element.173) | copy-start | bytes 1924
  448.7 16.1 %copy-start.17 = (pred[640]{0:T(1024)(128)(4,1)S(1)}, pred[640]{0:T(1024)(128)(4,1)}, u32[]{:S(2)}) copy-start(pred[640]{0:T(1024)(128)(4,1)} %get-tuple-element.174) | copy-start | bytes 1924
  448.7 16.1 %copy-start.18 = (pred[640]{0:T(1024)(128)(4,1)S(1)}, pred[640]{0:T(1024)(128)(4,1)}, u32[]{:S(2)}) copy-start(pred[640]{0:T(1024)(128)(4,1)} %get-tuple-element.175) | copy-start | bytes 1924
  448.7 16.1 %copy-start.19 = (pred[640]{0:T(1024)(128)(4,1)S(1)}, pred[640]{0:T(1024)(128)(4,1)}, u32[]{:S(2)}) copy-start(pred[640]{0:T(1024)(128)(4,1)} %get-tuple-element.176) | copy-start | bytes 1924
  738.9 138.3 %copy-start = (bf16[640,1024]{1,0:T(8,128)(2,1)S(1)}, bf16[640,1024]{1,0:T(8,128)(2,1)}, u32[]{:S(2)}) copy-start(bf16[640,1024]{1,0:T(8,128)(2,1)} %param.7) | copy-start | bytes 3932164
  (27 other events, 420.8 us)
Sparse Core Ops, SparseCore 0:
  9.1 383.6 all-gather.2
  394.6 336.7 all-gather.4
  739.0 138.1 reduce-scatter.1
